TPU v7x, 32 devices: a whole 2x2x4 slice. The times are simulated.
32 devices in a mesh: clips: 2 (over y), frame: 4 (over x, core), row: 4 (over z).
Axes of the slice: x: 2, y: 2, z: 4, core: 2. Of those that a mesh axis runs over, the one named last changes fastest.
Arguments:
- frames: bfloat16 [16, 512, 640], P(('clips', 'frame'), 'row'), parts along dimension 0, may hold values from -16 to 16
- key_index: int32 [4], P('clips'), parts along dimension 0, may hold values from 0 to 7, as said below
- w_query: bfloat16 [640, 640], replicated, may hold values from -0.25 to 0.25
- w_keyval: bfloat16 [640, 1280], replicated, may hold values from -0.25 to 0.25
- w_out: bfloat16 [640, 640], replicated, may hold values from -0.25 to 0.25
- norm_gain: float32 [640], replicated, may hold values from 0.1 to 1.9
- w_first: bfloat16 [3, 640, 640], replicated, may hold values from -0.125 to 0.125
- w_second: bfloat16 [3, 640, 640], replicated, may hold values from -0.125 to 0.125
Outputs:
- edited: bfloat16 [16, 512, 640], P(('clips', 'frame'), 'row'), parts along dimension 0
There are 2 independent parts, one for each index of `clips`. A program takes and returns all parts, laid end to end along the dimension named above; an argument that names none is the same for every part. Nothing has to cross between parts.
Inputs may be any that keep to these rules, and one draw needn't show every extreme that they name: `key_index`: two different frame indices of the window, in either order; one of them is the window's last frame 8 - 1.
All inputs are finite; a program needn't handle non-finite values.
Results may differ from a plain program's by a relative error of at most 0.0067.
Values may be sent and summed in bfloat16 or wider, within the bound.
No kernel may reach another device: no remote copies, remote signals or barrier semaphores. Data moves between devices by JAX's collectives and lax.ppermute only.
A program may use at most 128 MiB of HBM per device.

v0:
```python
from functools import partial
import jax
import jax.numpy as jnp
from jax import lax
from jax.sharding import PartitionSpec as P

HEADS = 10
HEAD_DIM = 64


def from_root(value, axis, source):
    kept = jnp.where(lax.axis_index(axis) == source, value, 0).astype(value.dtype)
    return lax.psum(kept, axis)


def extended(array, sides, width):
    for axis, dim in sides:
        size, length = (lax.axis_size(axis), array.shape[dim])
        up = [(i, (i + 1) % size) for i in range(size - 1)]
        down = [(j, i) for i, j in up]
        last = lax.slice_in_dim(array, length - width, length, axis=dim)
        first = lax.slice_in_dim(array, 0, width, axis=dim)
        before = lax.ppermute(last, axis, up)
        after = lax.ppermute(first, axis, down)
        array = jnp.concatenate([before, array, after], axis=dim)
    return array


def temporal_mix(padded, weights, count):
    result = jnp.zeros((count * padded.shape[1], padded.shape[2]), jnp.float32)
    for offset in range(3):
        window = padded[offset : offset + count].reshape(-1, padded.shape[2])
        result = result + jnp.dot(window, weights[offset], preferred_element_type=jnp.float32)
    return result


def absorb_keys(query_heads, channels, state_now, kv_pieces, piece_start):
    highest, denominator, accumulated = state_now
    joined = jnp.concatenate(kv_pieces, axis=0)
    key_heads = joined[:, :channels].reshape(-1, HEADS, HEAD_DIM)
    value_heads = joined[:, channels:].reshape(-1, HEADS, HEAD_DIM)
    scores = jnp.einsum(
        "qhd,khd->hqk", query_heads, key_heads, preferred_element_type=jnp.float32
    ) * HEAD_DIM ** (-0.5)
    raised = jnp.maximum(highest, jnp.max(scores, axis=-1))
    kept_frac = jnp.exp(highest - raised)
    exponent = jnp.exp(scores - raised[:, :, None])
    denominator = jnp.sum(exponent, axis=-1)
    contrib = jnp.einsum(
        "hqk,khd->qhd",
        exponent.astype(jnp.bfloat16),
        value_heads,
        preferred_element_type=jnp.float32,
    )
    accumulated = accumulated * jnp.repeat(kept_frac.T, HEAD_DIM, axis=1) + contrib.reshape(
        contrib.shape[0], -1
    )
    return (raised, denominator, accumulated)


def shards(frames, key_index, w_query, w_keyval, w_out, norm_gain, w_first, w_second):
    frame_count, row_count, channels = frames.shape
    flattened = frames.reshape(-1, channels)
    queries = jnp.dot(flattened, w_query, preferred_element_type=jnp.float32).astype(jnp.bfloat16)
    query_heads = queries.reshape(-1, HEADS, HEAD_DIM)
    query_total = queries.shape[0]
    owners = key_index // frame_count
    chosen = frames[key_index % frame_count].reshape(-1, channels)
    keyval = jnp.dot(chosen, w_keyval, preferred_element_type=jnp.float32).astype(jnp.bfloat16)
    own_parts = (keyval[:row_count], keyval[row_count:])
    initial = (
        jnp.full((HEADS, query_total), -1e30, jnp.float32),
        jnp.zeros((HEADS, query_total), jnp.float32),
        jnp.zeros((query_total, channels), jnp.float32),
    )
    absorb = partial(absorb_keys, query_heads, channels)
    spread_parts = []
    for key_slot in range(2):
        spread_parts.append(from_root(own_parts[key_slot], "frame", owners[key_slot]))
    final = absorb(
        initial,
        (
            lax.all_gather(spread_parts[0], "row", axis=0, tiled=True),
            lax.all_gather(spread_parts[1], "row", axis=0, tiled=True),
        ),
        jnp.int32(0),
    )
    highest, denominator, accumulated = final
    mixed = accumulated.reshape(query_total, HEADS, HEAD_DIM) / denominator.T[:, :, None]
    attended = mixed.reshape(query_total, channels).astype(jnp.bfloat16)
    residual = flattened.astype(jnp.float32) + jnp.dot(
        attended, w_out, preferred_element_type=jnp.float32
    )
    mean_square = jnp.mean(residual * residual, axis=-1, keepdims=True)
    normed = (residual * lax.rsqrt(mean_square + 1e-06) * norm_gain).astype(jnp.bfloat16)
    normed = normed.reshape(frame_count, row_count, channels)
    padded = extended(normed, (("frame", 0),), 1)
    hidden = jax.nn.silu(temporal_mix(padded, w_first, frame_count)).astype(jnp.bfloat16)
    hidden = hidden.reshape(frame_count, row_count, channels)
    padded = extended(hidden, (("frame", 0),), 1)
    second = temporal_mix(padded, w_second, frame_count)
    return (residual + second).astype(jnp.bfloat16).reshape(frame_count, row_count, channels)


def solution(mesh):
    return jax.shard_map(
        shards,
        mesh=mesh,
        in_specs=(P(("clips", "frame"), "row", None), P("clips"), P(), P(), P(), P(), P(), P()),
        out_specs=P(("clips", "frame"), "row", None),
        check_vma=False,
    )
```

profile of v0, /device:TPU:1, one launch (start us, length us, event | category | flops | bytes accessed | tf_op | source)
XLA Modules:
  0.0 162.4 jit_solution(13678371207064377667)
XLA Ops:
  6.5 0.8 and_select_fusion.1
  7.3 0.6 fusion.42
  9.2 1.6 gather_fusion
  10.8 0.7 convolution_convert_fusion
  11.5 0.9 slice_select_fusion
  12.5 34.7 %all-reduce.3.cloned.1.call-done = (bf16[128,1280]{1,0:T(8,128)(2,1)}, bf16[128,1280]{1,0:T(8,128)(2,1)}) async-done(((bf16[128,1280]{1,0:T(8,128)(2,1)}, bf16[128,1280]{1,0:T(8,128)(2,1)}), (bf16[128,1280]{1,0:T(8,128)(2,1)}, bf16[128,1280]{1,0:T(8,128)(2,1)})) %all-reduce.3.cloned.1.call-update) | async-done | bytes 655376 | tf_op jit(solution)/shard_map/psum | solution.py:13
  47.3 0.7 all-gather.5.cloned.1.call-update
  48.0 0.5 convolution_convert_fusion.1
  48.4 0.9 copy.12
  49.4 32.9 %all-gather.3.cloned.1.call-done = bf16[512,1280]{1,0:T(8,128)(2,1)} async-done(((bf16[128,1280]{1,0:T(8,128)(2,1)}), bf16[512,1280]{1,0:T(8,128)(2,1)}) %all-gather.3.cloned.1.call-update) | async-done | bytes 1310736 | tf_op jit(solution)/shard_map/all_gather | solution.py:83
  82.2 2.5 %constant_dynamic-update-slice_fusion.1 = bf16[1024,1280]{1,0:T(8,128)(2,1)} fusion(bf16[512,1280]{1,0:T(8,128)(2,1)} %all-gather.3.cloned.1.call-done), kind=kLoop, calls=%fused_computation.54 | loop fusion | bytes 2621440
  84.7 30.8 %all-gather.5.cloned.1.call-done = bf16[512,1280]{1,0:T(8,128)(2,1)} async-done(((bf16[128,1280]{1,0:T(8,128)(2,1)}), bf16[512,1280]{1,0:T(8,128)(2,1)}) %all-gather.5.cloned.1.call-update) | async-done | bytes 1310736 | tf_op jit(solution)/shard_map/all_gather | solution.py:84
  115.5 2.5 %constant_dynamic-update-slice_fusion = bf16[1024,1280]{1,0:T(8,128)(2,1)} fusion(bf16[1024,1280]{1,0:T(8,128)(2,1)} %constant_dynamic-update-slice_fusion.1, bf16[512,1280]{1,0:T(8,128)(2,1)} %all-gather.5.cloned.1.call-done), kind=kLoop, calls=%fused_computation.53 | loop fusion | bytes 2621440 | tf_op jit(solution)/shard_map/concatenate | solution.py:39
  118.0 3.5 %fusion.41 = (bf16[1024,640]{1,0:T(8,128)(2,1)}, bf16[1024,640]{1,0:T(8,128)(2,1)}) fusion(bf16[1024,1280]{1,0:T(8,128)(2,1)} %constant_dynamic-update-slice_fusion), kind=kLoop, calls=%fused_computation.63 | loop fusion | bytes 5242880 | tf_op jit(solution)/shard_map/slice | solution.py:40
  121.5 1.6 copy.13
  123.1 2.5 %copy.14 = bf16[1024,640]{0,1:T(8,128)(2,1)} copy(bf16[1024,640]{1,0:T(8,128)(2,1)} %get-tuple-element.8) | data formatting | bytes 2621440 | tf_op jit(solution)/shard_map/slice | solution.py:41
  125.5 2.6 %multiply_reduce_fusion = (f32[10,256]{1,0:T(8,128)S(1)}, f32[10,256,1024]{2,1,0:T(8,128)S(1)}) fusion(bf16[256,10,64]{0,2,1:T(8,128)(2,1)} %bitcast.74, bf16[1024,10,64]{0,2,1:T(8,128)(2,1)S(1)} %bitcast.69), kind=kOutput, calls=%fused_computation.2 | convolution fusion | flops 340784640 | bytes 12134400 | tf_op jit(solution)/shard_map/qhd,khd->hqk/dot_general | solution.py:42
  128.2 2.1 %fusion = f32[10,256]{1,0:T(8,128)S(1)} fusion(f32[10,256,1024]{2,1,0:T(8,128)S(1)} %get-tuple-element.26, f32[10,256]{1,0:T(8,128)S(1)} %get-tuple-element.20), kind=kLoop, calls=%fused_computation.3 | loop fusion | flops 7861760 | bytes 10506240 | tf_op jit(solution)/shard_map/reduce_sum | solution.py:48
  130.3 2.3 %fusion.19 = bf16[256,10,64]{0,2,1:T(8,128)(2,1)S(1)} fusion(bf16[1024,10,64]{0,2,1:T(8,128)(2,1)S(1)} %bitcast.77, f32[10,256,1024]{2,1,0:T(8,128)S(1)} %get-tuple-element.26, f32[10,256]{1,0:T(8,128)S(1)} %get-tuple-element.20, f32[256,10]{0,1:T(8,128)S(1)} %bitcast.82, f32[256,10]{0,1:T(8,128)S(1)} %get-tuple-element.19), kind=kOutput, calls=%fused_computation.20 | convolution fusion | flops 343900160 | bytes 12154880 | tf_op jit(solution)/shard_map/hqk,khd->qhd/dot_general | solution.py:49
  132.6 0.6 multiply_reduce_fusion.1
  133.4 4.3 %collective-permute-start = (bf16[1,128,640]{2,1,0:T(8,128)(2,1)S(1)}, bf16[1,128,640]{2,1,0:T(8,128)(2,1)S(1)}, u32[]{:S(2)}, u32[]{:S(2)}) collective-permute-start(bf16[1,128,640]{2,1,0:T(8,128)(2,1)S(1)} %get-tuple-element.17), channel_id=1, source_target_pairs={{0,4},{4,8},{8,12},{1,5},{5,9},{9,13},{2,6},{6,10},{10,14},{3,7},{... | collective-permute-start | bytes 491528 | tf_op jit(solution)/shard_map/ppermute | solution.py:23
  137.7 1.9 %collective-permute-start.1 = (bf16[1,128,640]{2,1,0:T(8,128)(2,1)S(1)}, bf16[1,128,640]{2,1,0:T(8,128)(2,1)S(1)}, u32[]{:S(2)}, u32[]{:S(2)}) collective-permute-start(bf16[1,128,640]{2,1,0:T(8,128)(2,1)S(1)} %get-tuple-element.18), channel_id=1, source_target_pairs={{4,0},{8,4},{12,8},{5,1},{9,5},{13,9},{6,2},{10,6},{14,10},{7,3},{... | collective-permute-start | bytes 491528 | tf_op jit(solution)/shard_map/ppermute | solution.py:24
  139.6 0.5 fusion.29
  140.1 4.2 %collective-permute-done.1 = bf16[1,128,640]{2,1,0:T(8,128)(2,1)S(1)} collective-permute-done((bf16[1,128,640]{2,1,0:T(8,128)(2,1)S(1)}, bf16[1,128,640]{2,1,0:T(8,128)(2,1)S(1)}, u32[]{:S(2)}, u32[]{:S(2)}) %collective-permute-start.1) | collective-permute-done | bytes 163872 | tf_op jit(solution)/shard_map/ppermute | solution.py:24
  144.4 0.5 fusion.27
  144.9 0.5 multiply_convert_fusion
  145.4 2.1 %collective-permute-start.2 = (bf16[1,128,640]{2,1,0:T(8,128)(2,1)S(1)}, bf16[1,128,640]{2,1,0:T(8,128)(2,1)S(1)}, u32[]{:S(2)}, u32[]{:S(2)}) collective-permute-start(bf16[1,128,640]{2,1,0:T(8,128)(2,1)S(1)} %get-tuple-element.13), channel_id=1, source_target_pairs={{0,4},{4,8},{8,12},{1,5},{5,9},{9,13},{2,6},{6,10},{10,14},{3,7},{... | collective-permute-start | bytes 491528 | tf_op jit(solution)/shard_map/ppermute | solution.py:23
  147.5 2.4 %collective-permute-start.3 = (bf16[1,128,640]{2,1,0:T(8,128)(2,1)S(1)}, bf16[1,128,640]{2,1,0:T(8,128)(2,1)S(1)}, u32[]{:S(2)}, u32[]{:S(2)}) collective-permute-start(bf16[1,128,640]{2,1,0:T(8,128)(2,1)S(1)} %get-tuple-element.14), channel_id=1, source_target_pairs={{4,0},{8,4},{12,8},{5,1},{9,5},{13,9},{6,2},{10,6},{14,10},{7,3},{... | collective-permute-start | bytes 491528 | tf_op jit(solution)/shard_map/ppermute | solution.py:24
  149.9 0.5 fusion.24
  150.4 3.7 %collective-permute-done.3 = bf16[1,128,640]{2,1,0:T(8,128)(2,1)S(1)} collective-permute-done((bf16[1,128,640]{2,1,0:T(8,128)(2,1)S(1)}, bf16[1,128,640]{2,1,0:T(8,128)(2,1)S(1)}, u32[]{:S(2)}, u32[]{:S(2)}) %collective-permute-start.3) | collective-permute-done | bytes 163872 | tf_op jit(solution)/shard_map/ppermute | solution.py:24
  154.2 0.5 fusion.22
  154.7 1.2 fusion.15
  (31 shorter events, 0.5 us)
Async XLA Ops:
  6.5 4.3 %copy-start = (bf16[640,1280]{1,0:T(8,128)(2,1)S(1)}, bf16[640,1280]{1,0:T(8,128)(2,1)}, u32[]{:S(2)}) copy-start(bf16[640,1280]{1,0:T(8,128)(2,1)} %param.11) | copy-start | bytes 4915204
  6.5 40.7 %all-reduce.3.cloned.1.call-start = ((), (), s32[]{:S(2)}) async-start(), calls=%async_computation.2 | async-start | bytes 1310720 | tf_op jit(solution)/shard_map/psum | solution.py:13
  10.8 37.2 %copy-start.1 = (bf16[2,128,640]{2,1,0:T(8,128)(2,1)S(1)}, bf16[2,128,640]{2,1,0:T(8,128)(2,1)}, u32[]{:S(2)}) copy-start(bf16[2,128,640]{2,1,0:T(8,128)(2,1)} %param.8) | copy-start | bytes 983044
  10.8 37.2 %copy-start.5 = (bf16[640,640]{1,0:T(8,128)(2,1)S(1)}, bf16[640,640]{1,0:T(8,128)(2,1)}, u32[]{:S(2)}) copy-start(bf16[640,640]{1,0:T(8,128)(2,1)} %param.10) | copy-start | bytes 2457604
  12.5 69.8 %all-gather.3.cloned.1.call-start = ((), (), s32[]{:S(2)}) async-start(), calls=%async_computation | async-start | bytes 1638400 | tf_op jit(solution)/shard_map/all_gather | solution.py:83
  47.2 68.3 %all-gather.5.cloned.1.call-start = ((), (), s32[]{:S(2)}) async-start(), calls=%async_computation.1 | async-start | bytes 1638400 | tf_op jit(solution)/shard_map/all_gather | solution.py:84
  128.2 2.1 %copy-start.3 = (bf16[1024,640]{0,1:T(8,128)(2,1)S(1)}, bf16[1024,640]{0,1:T(8,128)(2,1)}, u32[]{:S(2)}) copy-start(bf16[1024,640]{0,1:T(8,128)(2,1)} %copy.14) | copy-start | bytes 3932164
  130.2 2.3 %copy-start.6 = (bf16[640,640]{1,0:T(8,128)(2,1)S(1)}, bf16[640,640]{1,0:T(8,128)(2,1)}, u32[]{:S(2)}) copy-start(bf16[640,640]{1,0:T(8,128)(2,1)} %param.12) | copy-start | bytes 2457604
  130.3 2.9 %copy-start.7 = (f32[640]{0:T(1024)S(1)}, f32[640]{0:T(1024)}, u32[]{:S(2)}) copy-start(f32[640]{0:T(1024)} %param.13) | copy-start | bytes 7684
  132.6 7.1 %copy-start.4 = (bf16[3,640,640]{2,1,0:T(8,128)(2,1)S(1)}, bf16[3,640,640]{2,1,0:T(8,128)(2,1)}, u32[]{:S(2)}) copy-start(bf16[3,640,640]{2,1,0:T(8,128)(2,1)} %param.14) | copy-start | bytes 7372804
  133.4 6.7 %collective-permute-start = (bf16[1,128,640]{2,1,0:T(8,128)(2,1)S(1)}, bf16[1,128,640]{2,1,0:T(8,128)(2,1)S(1)}, u32[]{:S(2)}, u32[]{:S(2)}) collective-permute-start(bf16[1,128,640]{2,1,0:T(8,128)(2,1)S(1)} %get-tuple-element.17), channel_id=1, source_target_pairs={{0,4},{4,8},{8,12},{1,5},{5,9},{9,13},{2,6},{6,10},{10,14},{3,7},{... | collective-permute-start | bytes 491528 | tf_op jit(solution)/shard_map/ppermute | solution.py:23
  137.7 6.6 %collective-permute-start.1 = (bf16[1,128,640]{2,1,0:T(8,128)(2,1)S(1)}, bf16[1,128,640]{2,1,0:T(8,128)(2,1)S(1)}, u32[]{:S(2)}, u32[]{:S(2)}) collective-permute-start(bf16[1,128,640]{2,1,0:T(8,128)(2,1)S(1)} %get-tuple-element.18), channel_id=1, source_target_pairs={{4,0},{8,4},{12,8},{5,1},{9,5},{13,9},{6,2},{10,6},{14,10},{7,3},{... | collective-permute-start | bytes 491528 | tf_op jit(solution)/shard_map/ppermute | solution.py:24
  144.9 5.1 %copy-start.2 = (bf16[3,640,640]{2,1,0:T(8,128)(2,1)S(1)}, bf16[3,640,640]{2,1,0:T(8,128)(2,1)}, u32[]{:S(2)}) copy-start(bf16[3,640,640]{2,1,0:T(8,128)(2,1)} %param.15) | copy-start | bytes 7372804
  145.4 5.0 %collective-permute-start.2 = (bf16[1,128,640]{2,1,0:T(8,128)(2,1)S(1)}, bf16[1,128,640]{2,1,0:T(8,128)(2,1)S(1)}, u32[]{:S(2)}, u32[]{:S(2)}) collective-permute-start(bf16[1,128,640]{2,1,0:T(8,128)(2,1)S(1)} %get-tuple-element.13), channel_id=1, source_target_pairs={{0,4},{4,8},{8,12},{1,5},{5,9},{9,13},{2,6},{6,10},{10,14},{3,7},{... | collective-permute-start | bytes 491528 | tf_op jit(solution)/shard_map/ppermute | solution.py:23
  147.5 6.6 %collective-permute-start.3 = (bf16[1,128,640]{2,1,0:T(8,128)(2,1)S(1)}, bf16[1,128,640]{2,1,0:T(8,128)(2,1)S(1)}, u32[]{:S(2)}, u32[]{:S(2)}) collective-permute-start(bf16[1,128,640]{2,1,0:T(8,128)(2,1)S(1)} %get-tuple-element.14), channel_id=1, source_target_pairs={{4,0},{8,4},{12,8},{5,1},{9,5},{13,9},{6,2},{10,6},{14,10},{7,3},{... | collective-permute-start | bytes 491528 | tf_op jit(solution)/shard_map/ppermute | solution.py:24
Sparse Core Ops, SparseCore 0:
  12.6 34.5 all-reduce.2
  48.8 33.4 all-gather.2
  83.8 31.6 all-gather.4
where the time goes:
time: 163 us; the launch traced here: 162 us
  waiting for transfers between devices  107 us (66%)
  local copies, waits for them, and re-layouts  15.6 us (10%)
  between operations  14.7 us (9%)
  starting transfers between devices  10.8 us (7%)
  matrix products  10.2 us (6%)
  other arithmetic  4.05 us (2%)
    psum x1, waiting for transfers between devices, from_root(): return lax.psum(kept, axis)  34.7 us
    all_gather x1, waiting for transfers between devices, shards(): lax.all_gather(spread_parts[0], 'row', axis=0, tiled=True)  32.9 us
    all_gather x1, waiting for transfers between devices, shards(): lax.all_gather(spread_parts[1], 'row', axis=0, tiled=True)  30.8 us
    ppermute x2, waiting for transfers between devices, extended(): after = lax.ppermute(first, axis, down)  7.96 us
    ppermute x2, starting transfers between devices, extended(): before = lax.ppermute(last, axis, up)  6.37 us
    slice x2, local copies, waits for them, and re-layouts, absorb_keys(): key_heads = joined[:, :channels].reshape(-1, HEADS, HEAD_DIM)  5.06 us
    ppermute x2, starting transfers between devices, extended(): after = lax.ppermute(first, axis, down)  4.33 us
    dot_general x6, matrix products, temporal_mix(): jnp.dot(window, weights[offset], preferred_element_type=jnp.float32)  3.53 us
  transfers between devices with their start and end apart: 7, of which 5 were waited for; matrix products, arithmetic and copies ran while one was open for 3% of the time, Pallas kernels for 0%

commit v1 on v0

--- a/solution.py
+++ b/solution.py
@@ -10,7 +10,12 @@
 
 def from_root(value, axis, source):
     kept = jnp.where(lax.axis_index(axis) == source, value, 0).astype(value.dtype)
-    return lax.psum(kept, axis)
+
+    def links_launch(x0):
+        item_now = jnp.sum(lax.all_gather(x0, axis), axis=0)
+        return item_now
+
+    return links_launch(kept)
 
 
 def extended(array, sides, width):

time: 163 us -> 167 us (1.025)
  other arithmetic: 4.05 us -> 8.68 us
    all_gather x0 -> x2, waiting for transfers between devices: none -> 37.4 us  [links_launch(): item_now = jnp.sum(lax.all_gather(x0, axis), axis=0)]
    psum x1 -> x0, waiting for transfers between devices: 34.7 us -> none  [from_root(): return lax.psum(kept, axis)]
    reduce_sum x0 -> x2, other arithmetic: none -> 4.64 us  [links_launch(): item_now = jnp.sum(lax.all_gather(x0, axis), axis=0)]
    all_gather x1, waiting for transfers between devices: 32.9 us -> 29.5 us  [shards(): lax.all_gather(spread_parts[0], 'row', axis=0, tiled=True)]
  transfers between devices with their start and end apart: 7 -> 8, of which waited for: 5 -> 6; matrix products, arithmetic and copies ran while one was open for 3% -> 6% of each run, Pallas kernels for 0% -> 0%
where the time goes in v1:
time: 167 us; the launch traced here: 166 us
  waiting for transfers between devices  106 us (63%)
  local copies, waits for them, and re-layouts  15.7 us (9%)
  between operations  14.6 us (9%)
  starting transfers between devices  10.8 us (6%)
  matrix products  10.2 us (6%)
  other arithmetic  8.68 us (5%)
    all_gather x2, waiting for transfers between devices, links_launch(): item_now = jnp.sum(lax.all_gather(x0, axis), axis=0)  37.4 us
    all_gather x1, waiting for transfers between devices, shards(): lax.all_gather(spread_parts[1], 'row', axis=0, tiled=True)  30.7 us
    all_gather x1, waiting for transfers between devices, shards(): lax.all_gather(spread_parts[0], 'row', axis=0, tiled=True)  29.5 us
    ppermute x2, waiting for transfers between devices, extended(): after = lax.ppermute(first, axis, down)  7.96 us
    ppermute x2, starting transfers between devices, extended(): before = lax.ppermute(last, axis, up)  6.37 us
    slice x2, local copies, waits for them, and re-layouts, absorb_keys(): key_heads = joined[:, :channels].reshape(-1, HEADS, HEAD_DIM)  5.06 us
    reduce_sum x2, other arithmetic, links_launch(): item_now = jnp.sum(lax.all_gather(x0, axis), axis=0)  4.64 us
    ppermute x2, starting transfers between devices, extended(): after = lax.ppermute(first, axis, down)  4.33 us
  transfers between devices with their start and end apart: 8, of which 6 were waited for; matrix products, arithmetic and copies ran while one was open for 6% of the time, Pallas kernels for 0%

profile of v1, /device:TPU:1, one launch (start us, length us, event | category | flops | bytes accessed | tf_op | source)
XLA Modules:
  0.0 166.3 jit_solution(2893601016496983775)
XLA Ops:
  6.5 0.8 and_select_fusion.1
  7.3 0.6 fusion.42
  9.1 1.6 gather_fusion
  10.7 0.7 convolution_convert_fusion
  11.4 0.9 slice_select_fusion
  12.4 0.7 all-gather.13.cloned.1.call-update
  13.1 20.0 %all-gather.11.cloned.1.call-done = bf16[512,1280]{1,0:T(8,128)(2,1)} async-done(((bf16[128,1280]{1,0:T(8,128)(2,1)}), bf16[512,1280]{1,0:T(8,128)(2,1)}) %all-gather.11.cloned.1.call-update) | async-done | bytes 1310736 | tf_op jit(solution)/shard_map/all_gather | solution.py:15
  33.2 2.3 %reduce_sum.42 = bf16[128,1280]{1,0:T(8,128)(2,1)} reduce(bf16[4,128,1280]{2,1,0:T(8,128)(2,1)} %bitcast.80, bf16[]{:T(256)} %constant.48.clone.1), dimensions={0}, to_apply=%region_0.1 | reduce | flops 491520 | bytes 1638402 | tf_op jit(solution)/shard_map/reduce_sum | solution.py:15
  35.6 17.4 %all-gather.13.cloned.1.call-done = bf16[512,1280]{1,0:T(8,128)(2,1)} async-done(((bf16[128,1280]{1,0:T(8,128)(2,1)}), bf16[512,1280]{1,0:T(8,128)(2,1)}) %all-gather.13.cloned.1.call-update) | async-done | bytes 1310736 | tf_op jit(solution)/shard_map/all_gather | solution.py:15
  53.0 2.3 %reduce_sum.43 = bf16[128,1280]{1,0:T(8,128)(2,1)} reduce(bf16[4,128,1280]{2,1,0:T(8,128)(2,1)} %bitcast.79, bf16[]{:T(256)} %constant.48.clone.1), dimensions={0}, to_apply=%region_1.2 | reduce | flops 491520 | bytes 1638402 | tf_op jit(solution)/shard_map/reduce_sum | solution.py:15
  55.3 0.5 convolution_convert_fusion.1
  55.8 0.9 copy.11
  56.7 29.5 %all-gather.7.cloned.1.call-done = bf16[512,1280]{1,0:T(8,128)(2,1)} async-done(((bf16[128,1280]{1,0:T(8,128)(2,1)}), bf16[512,1280]{1,0:T(8,128)(2,1)}) %all-gather.7.cloned.1.call-update) | async-done | bytes 1310736 | tf_op jit(solution)/shard_map/all_gather | solution.py:88
  86.2 2.5 %constant_dynamic-update-slice_fusion.1 = bf16[1024,1280]{1,0:T(8,128)(2,1)} fusion(bf16[512,1280]{1,0:T(8,128)(2,1)} %all-gather.7.cloned.1.call-done), kind=kLoop, calls=%fused_computation.54 | loop fusion | bytes 2621440
  88.7 30.7 %all-gather.9.cloned.1.call-done = bf16[512,1280]{1,0:T(8,128)(2,1)} async-done(((bf16[128,1280]{1,0:T(8,128)(2,1)}), bf16[512,1280]{1,0:T(8,128)(2,1)}) %all-gather.9.cloned.1.call-update) | async-done | bytes 1310736 | tf_op jit(solution)/shard_map/all_gather | solution.py:89
  119.4 2.5 %constant_dynamic-update-slice_fusion = bf16[1024,1280]{1,0:T(8,128)(2,1)} fusion(bf16[1024,1280]{1,0:T(8,128)(2,1)} %constant_dynamic-update-slice_fusion.1, bf16[512,1280]{1,0:T(8,128)(2,1)} %all-gather.9.cloned.1.call-done), kind=kLoop, calls=%fused_computation.53 | loop fusion | bytes 2621440 | tf_op jit(solution)/shard_map/concatenate | solution.py:44
  121.8 3.5 %fusion.41 = (bf16[1024,640]{1,0:T(8,128)(2,1)}, bf16[1024,640]{1,0:T(8,128)(2,1)}) fusion(bf16[1024,1280]{1,0:T(8,128)(2,1)} %constant_dynamic-update-slice_fusion), kind=kLoop, calls=%fused_computation.63 | loop fusion | bytes 5242880 | tf_op jit(solution)/shard_map/slice | solution.py:45
  125.3 1.6 copy.12
  126.9 2.5 %copy.13 = bf16[1024,640]{0,1:T(8,128)(2,1)} copy(bf16[1024,640]{1,0:T(8,128)(2,1)} %get-tuple-element.6) | data formatting | bytes 2621440 | tf_op jit(solution)/shard_map/slice | solution.py:46
  129.4 2.6 %multiply_reduce_fusion = (f32[10,256]{1,0:T(8,128)S(1)}, f32[10,256,1024]{2,1,0:T(8,128)S(1)}) fusion(bf16[256,10,64]{0,2,1:T(8,128)(2,1)} %bitcast.76, bf16[1024,10,64]{0,2,1:T(8,128)(2,1)S(1)} %bitcast.71), kind=kOutput, calls=%fused_computation.2 | convolution fusion | flops 340784640 | bytes 12134400 | tf_op jit(solution)/shard_map/qhd,khd->hqk/dot_general | solution.py:47
  132.0 2.1 %fusion = f32[10,256]{1,0:T(8,128)S(1)} fusion(f32[10,256,1024]{2,1,0:T(8,128)S(1)} %get-tuple-element.24, f32[10,256]{1,0:T(8,128)S(1)} %get-tuple-element.18), kind=kLoop, calls=%fused_computation.3 | loop fusion | flops 7861760 | bytes 10506240 | tf_op jit(solution)/shard_map/reduce_sum | solution.py:53
  134.1 2.3 %fusion.19 = bf16[256,10,64]{0,2,1:T(8,128)(2,1)S(1)} fusion(bf16[1024,10,64]{0,2,1:T(8,128)(2,1)S(1)} %bitcast.81, f32[10,256,1024]{2,1,0:T(8,128)S(1)} %get-tuple-element.24, f32[10,256]{1,0:T(8,128)S(1)} %get-tuple-element.18, f32[256,10]{0,1:T(8,128)S(1)} %bitcast.86, f32[256,10]{0,1:T(8,128)S(1)} %get-tuple-element.17), kind=kOutput, calls=%fused_computation.20 | convolution fusion | flops 343900160 | bytes 12154880 | tf_op jit(solution)/shard_map/hqk,khd->qhd/dot_general | solution.py:54
  136.5 0.6 multiply_reduce_fusion.1
  137.2 4.3 %collective-permute-start = (bf16[1,128,640]{2,1,0:T(8,128)(2,1)S(1)}, bf16[1,128,640]{2,1,0:T(8,128)(2,1)S(1)}, u32[]{:S(2)}, u32[]{:S(2)}) collective-permute-start(bf16[1,128,640]{2,1,0:T(8,128)(2,1)S(1)} %get-tuple-element.15), channel_id=1, source_target_pairs={{0,4},{4,8},{8,12},{1,5},{5,9},{9,13},{2,6},{6,10},{10,14},{3,7},{... | collective-permute-start | bytes 491528 | tf_op jit(solution)/shard_map/ppermute | solution.py:28
  141.6 1.9 %collective-permute-start.1 = (bf16[1,128,640]{2,1,0:T(8,128)(2,1)S(1)}, bf16[1,128,640]{2,1,0:T(8,128)(2,1)S(1)}, u32[]{:S(2)}, u32[]{:S(2)}) collective-permute-start(bf16[1,128,640]{2,1,0:T(8,128)(2,1)S(1)} %get-tuple-element.16), channel_id=1, source_target_pairs={{4,0},{8,4},{12,8},{5,1},{9,5},{13,9},{6,2},{10,6},{14,10},{7,3},{... | collective-permute-start | bytes 491528 | tf_op jit(solution)/shard_map/ppermute | solution.py:29
  144.0 4.2 %collective-permute-done.1 = bf16[1,128,640]{2,1,0:T(8,128)(2,1)S(1)} collective-permute-done((bf16[1,128,640]{2,1,0:T(8,128)(2,1)S(1)}, bf16[1,128,640]{2,1,0:T(8,128)(2,1)S(1)}, u32[]{:S(2)}, u32[]{:S(2)}) %collective-permute-start.1) | collective-permute-done | bytes 163872 | tf_op jit(solution)/shard_map/ppermute | solution.py:29
  148.7 0.5 multiply_convert_fusion
  149.3 2.1 %collective-permute-start.2 = (bf16[1,128,640]{2,1,0:T(8,128)(2,1)S(1)}, bf16[1,128,640]{2,1,0:T(8,128)(2,1)S(1)}, u32[]{:S(2)}, u32[]{:S(2)}) collective-permute-start(bf16[1,128,640]{2,1,0:T(8,128)(2,1)S(1)} %get-tuple-element.11), channel_id=1, source_target_pairs={{0,4},{4,8},{8,12},{1,5},{5,9},{9,13},{2,6},{6,10},{10,14},{3,7},{... | collective-permute-start | bytes 491528 | tf_op jit(solution)/shard_map/ppermute | solution.py:28
  151.4 2.4 %collective-permute-start.3 = (bf16[1,128,640]{2,1,0:T(8,128)(2,1)S(1)}, bf16[1,128,640]{2,1,0:T(8,128)(2,1)S(1)}, u32[]{:S(2)}, u32[]{:S(2)}) collective-permute-start(bf16[1,128,640]{2,1,0:T(8,128)(2,1)S(1)} %get-tuple-element.12), channel_id=1, source_target_pairs={{4,0},{8,4},{12,8},{5,1},{9,5},{13,9},{6,2},{10,6},{14,10},{7,3},{... | collective-permute-start | bytes 491528 | tf_op jit(solution)/shard_map/ppermute | solution.py:29
  153.8 0.5 fusion.24
  154.3 3.7 %collective-permute-done.3 = bf16[1,128,640]{2,1,0:T(8,128)(2,1)S(1)} collective-permute-done((bf16[1,128,640]{2,1,0:T(8,128)(2,1)S(1)}, bf16[1,128,640]{2,1,0:T(8,128)(2,1)S(1)}, u32[]{:S(2)}, u32[]{:S(2)}) %collective-permute-start.3) | collective-permute-done | bytes 163872 | tf_op jit(solution)/shard_map/ppermute | solution.py:29
  158.5 1.2 fusion.15
  (36 shorter events, 1.9 us)
Async XLA Ops:
  6.5 4.2 %copy-start = (bf16[640,1280]{1,0:T(8,128)(2,1)S(1)}, bf16[640,1280]{1,0:T(8,128)(2,1)}, u32[]{:S(2)}) copy-start(bf16[640,1280]{1,0:T(8,128)(2,1)} %param.11) | copy-start | bytes 4915204
  6.5 26.6 %all-gather.11.cloned.1.call-start = ((), (), s32[]{:S(2)}) async-start(), calls=%async_computation.2 | async-start | bytes 1638400 | tf_op jit(solution)/shard_map/all_gather | solution.py:15
  12.3 43.0 %copy-start.1 = (bf16[2,128,640]{2,1,0:T(8,128)(2,1)S(1)}, bf16[2,128,640]{2,1,0:T(8,128)(2,1)}, u32[]{:S(2)}) copy-start(bf16[2,128,640]{2,1,0:T(8,128)(2,1)} %param.8) | copy-start | bytes 983044
  12.3 43.0 %copy-start.5 = (bf16[640,640]{1,0:T(8,128)(2,1)S(1)}, bf16[640,640]{1,0:T(8,128)(2,1)}, u32[]{:S(2)}) copy-start(bf16[640,640]{1,0:T(8,128)(2,1)} %param.10) | copy-start | bytes 2457604
  12.4 40.6 %all-gather.13.cloned.1.call-start = ((), (), s32[]{:S(2)}) async-start(), calls=%async_computation.3 | async-start | bytes 1638400 | tf_op jit(solution)/shard_map/all_gather | solution.py:15
  13.1 73.1 %all-gather.7.cloned.1.call-start = ((), (), s32[]{:S(2)}) async-start(), calls=%async_computation | async-start | bytes 1638400 | tf_op jit(solution)/shard_map/all_gather | solution.py:88
  35.5 83.8 %all-gather.9.cloned.1.call-start = ((), (), s32[]{:S(2)}) async-start(), calls=%async_computation.1 | async-start | bytes 1638400 | tf_op jit(solution)/shard_map/all_gather | solution.py:89
  132.0 2.1 %copy-start.3 = (bf16[1024,640]{0,1:T(8,128)(2,1)S(1)}, bf16[1024,640]{0,1:T(8,128)(2,1)}, u32[]{:S(2)}) copy-start(bf16[1024,640]{0,1:T(8,128)(2,1)} %copy.13) | copy-start | bytes 3932164
  134.1 2.3 %copy-start.6 = (bf16[640,640]{1,0:T(8,128)(2,1)S(1)}, bf16[640,640]{1,0:T(8,128)(2,1)}, u32[]{:S(2)}) copy-start(bf16[640,640]{1,0:T(8,128)(2,1)} %param.12) | copy-start | bytes 2457604
  134.1 2.9 %copy-start.7 = (f32[640]{0:T(1024)S(1)}, f32[640]{0:T(1024)}, u32[]{:S(2)}) copy-start(f32[640]{0:T(1024)} %param.13) | copy-start | bytes 7684
  136.4 7.1 %copy-start.4 = (bf16[3,640,640]{2,1,0:T(8,128)(2,1)S(1)}, bf16[3,640,640]{2,1,0:T(8,128)(2,1)}, u32[]{:S(2)}) copy-start(bf16[3,640,640]{2,1,0:T(8,128)(2,1)} %param.14) | copy-start | bytes 7372804
  137.2 6.7 %collective-permute-start = (bf16[1,128,640]{2,1,0:T(8,128)(2,1)S(1)}, bf16[1,128,640]{2,1,0:T(8,128)(2,1)S(1)}, u32[]{:S(2)}, u32[]{:S(2)}) collective-permute-start(bf16[1,128,640]{2,1,0:T(8,128)(2,1)S(1)} %get-tuple-element.15), channel_id=1, source_target_pairs={{0,4},{4,8},{8,12},{1,5},{5,9},{9,13},{2,6},{6,10},{10,14},{3,7},{... | collective-permute-start | bytes 491528 | tf_op jit(solution)/shard_map/ppermute | solution.py:28
  141.6 6.6 %collective-permute-start.1 = (bf16[1,128,640]{2,1,0:T(8,128)(2,1)S(1)}, bf16[1,128,640]{2,1,0:T(8,128)(2,1)S(1)}, u32[]{:S(2)}, u32[]{:S(2)}) collective-permute-start(bf16[1,128,640]{2,1,0:T(8,128)(2,1)S(1)} %get-tuple-element.16), channel_id=1, source_target_pairs={{4,0},{8,4},{12,8},{5,1},{9,5},{13,9},{6,2},{10,6},{14,10},{7,3},{... | collective-permute-start | bytes 491528 | tf_op jit(solution)/shard_map/ppermute | solution.py:29
  148.7 5.1 %copy-start.2 = (bf16[3,640,640]{2,1,0:T(8,128)(2,1)S(1)}, bf16[3,640,640]{2,1,0:T(8,128)(2,1)}, u32[]{:S(2)}) copy-start(bf16[3,640,640]{2,1,0:T(8,128)(2,1)} %param.15) | copy-start | bytes 7372804
  149.3 5.0 %collective-permute-start.2 = (bf16[1,128,640]{2,1,0:T(8,128)(2,1)S(1)}, bf16[1,128,640]{2,1,0:T(8,128)(2,1)S(1)}, u32[]{:S(2)}, u32[]{:S(2)}) collective-permute-start(bf16[1,128,640]{2,1,0:T(8,128)(2,1)S(1)} %get-tuple-element.11), channel_id=1, source_target_pairs={{0,4},{4,8},{8,12},{1,5},{5,9},{9,13},{2,6},{6,10},{10,14},{3,7},{... | collective-permute-start | bytes 491528 | tf_op jit(solution)/shard_map/ppermute | solution.py:28
  151.4 6.6 %collective-permute-start.3 = (bf16[1,128,640]{2,1,0:T(8,128)(2,1)S(1)}, bf16[1,128,640]{2,1,0:T(8,128)(2,1)S(1)}, u32[]{:S(2)}, u32[]{:S(2)}) collective-permute-start(bf16[1,128,640]{2,1,0:T(8,128)(2,1)S(1)} %get-tuple-element.12), channel_id=1, source_target_pairs={{4,0},{8,4},{12,8},{5,1},{9,5},{13,9},{6,2},{10,6},{14,10},{7,3},{... | collective-permute-start | bytes 491528 | tf_op jit(solution)/shard_map/ppermute | solution.py:29
Sparse Core Ops, SparseCore 0:
  12.5 20.6 all-gather.10
  34.7 18.1 all-gather.12
  54.5 31.6 all-gather.6
  87.6 31.6 all-gather.8
